TPU v7x, 512 devices: a whole 4x8x8 slice. The times are simulated.
512 devices in a mesh: fsdp: 16 (over y, core), expert: 32 (over x, z).
Axes of the slice: x: 4, y: 8, z: 8, core: 2. Of those that a mesh axis runs over, the one named last changes fastest.
Arguments:
- frames: bfloat16 [16, 4096, 1536], P('fsdp', 'expert'), may hold values from -6 to 6
- ln_gain: float32 [1536], replicated, may hold values from 0.5 to 1.5
- kernel: float32 [31, 1536], replicated, may hold values from -1 to 1
- bn_scale: float32 [1536], replicated, may hold values from 0.5 to 2
- bn_shift: float32 [1536], replicated, may hold values from -1 to 1
- ffn_gain: float32 [1536], replicated, may hold values from 0.5 to 1.5
- expert_ids: int32 [16, 4096, 2], P('fsdp', 'expert'), may hold values from 0 to 31, all different within a row; in each aligned block of 128 rows (0 to 127, 128 to 255, ..., all dimensions but the last counted through in order) at most 16 rows name the same one
- gates: float32 [16, 4096, 2], P('fsdp', 'expert'), may hold values from 0.1 to 1
- w_in: bfloat16 [32, 1536, 1536], P('expert', 'fsdp'), may hold values from -0.15625 to 0.15625
- w_out: bfloat16 [32, 1536, 1536], P('expert', 'fsdp'), may hold values from -0.15625 to 0.15625
Outputs:
- layer_out: bfloat16 [16, 4096, 1536], P('fsdp', 'expert')
Inputs may be any that keep to these rules, and one draw needn't show every extreme that they name: `expert_ids`: the 2 experts of a frame differ; within the 128 frames of one device (aligned blocks along a sequence) no expert is named more than 16 times, a bound that some block reaches.
All inputs are finite; a program needn't handle non-finite values.
Results may differ from a plain program's by a relative error of at most 0.0039.
Values may be sent and summed in bfloat16 or wider, within the bound.
No kernel may reach another device: no remote copies, remote signals or barrier semaphores. Data moves between devices by JAX's collectives and lax.ppermute only.
A program may use at most 64 MiB of HBM per device.

v0:
```python
import jax
import jax.numpy as jnp
from jax import lax
from jax.sharding import PartitionSpec as P

eps_norm = 1e-05


def padded_2(block, sides, width):
    for axis, dim in sides:
        count = lax.axis_size(axis)
        forward = [(i, i + 1) for i in range(count - 1)]
        backward = [(target, source) for source, target in forward]
        low = lax.ppermute(
            lax.slice_in_dim(block, block.shape[dim] - width, None, axis=dim), axis, forward
        )
        high = lax.ppermute(lax.slice_in_dim(block, 0, width, axis=dim), axis, backward)
        block = jnp.concatenate([low, block, high], axis=dim)
    return block


def layer_norm(values, gain):
    centre = jnp.mean(values, axis=-1, keepdims=True)
    centred = values - centre
    spread = jnp.mean(centred * centred, axis=-1, keepdims=True)
    return centred * lax.rsqrt(spread + eps_norm) * gain


def shards(frames, ln_gain, kernel, bn_scale, bn_shift, ffn_gain, expert_ids, gates, w_in, w_out):
    frame_count = frames.shape[1]
    width = frames.shape[2]
    taps = kernel.shape[0]
    reach = (taps - 1) // 2
    picks_per = expert_ids.shape[2]
    experts_all = lax.axis_size("expert") * w_in.shape[0]
    capacity = 2 * picks_per * frame_count // experts_all
    slots_all = experts_all * capacity
    stream = frames[0].astype(jnp.float32)
    normed = layer_norm(stream, ln_gain).astype(jnp.bfloat16)
    padded = padded_2(normed, (("expert", 0),), reach)
    filtered = jnp.zeros(stream.shape, jnp.float32)
    for offset in range(taps):
        filtered = filtered + kernel[offset] * padded[offset : offset + frame_count]
    mixed = stream + jax.nn.silu(bn_scale * filtered + bn_shift)
    routed = layer_norm(mixed, ffn_gain).astype(jnp.bfloat16)
    chosen = expert_ids[0].reshape(-1)
    onehot = (chosen[:, None] == jnp.arange(experts_all, dtype=jnp.int32)[None, :]).astype(
        jnp.int32
    )
    before = jnp.cumsum(onehot, axis=0) - onehot
    slot_at = jnp.sum(before * onehot, axis=1)
    target = (chosen * capacity + slot_at).reshape(frame_count, picks_per)
    placing = jnp.any(
        target[None, :, :] == jnp.arange(slots_all, dtype=jnp.int32)[:, None, None], axis=2
    )
    outgoing = jnp.dot(placing.astype(jnp.bfloat16), routed, preferred_element_type=jnp.float32)
    outgoing = outgoing.astype(jnp.bfloat16).reshape(experts_all, capacity, width)
    full_in, full_out = (
        lax.all_gather(w_in, "fsdp", axis=1, tiled=True),
        lax.all_gather(w_out, "fsdp", axis=1, tiled=True),
    )
    block = lax.all_to_all(outgoing, "expert", split_axis=0, concat_axis=0, tiled=True)
    rows_in = block.reshape(-1, width)
    hidden = jax.nn.silu(jnp.dot(rows_in, full_in[0], preferred_element_type=jnp.float32)).astype(
        jnp.bfloat16
    )
    result = jnp.dot(hidden, full_out[0], preferred_element_type=jnp.float32).astype(jnp.bfloat16)
    returned = lax.all_to_all(
        result.reshape(block.shape), "expert", split_axis=0, concat_axis=0, tiled=True
    )
    rows_back = returned.reshape(-1, width)
    picked = (
        jnp.take(rows_back, target.reshape(-1), axis=0)
        .reshape(frame_count, picks_per, width)
        .astype(jnp.float32)
    )
    combined = jnp.sum(gates[0][:, :, None] * picked, axis=1)
    return (mixed + 0.5 * combined).astype(jnp.bfloat16)[None]


def solution(mesh):
    return jax.shard_map(
        shards,
        mesh=mesh,
        in_specs=(
            P("fsdp", "expert", None),
            P(),
            P(),
            P(),
            P(),
            P(),
            P("fsdp", "expert", None),
            P("fsdp", "expert", None),
            P("expert", "fsdp", None),
            P("expert", "fsdp", None),
        ),
        out_specs=P("fsdp", "expert", None),
        check_vma=False,
    )
```

profile of v0, /device:TPU:8, one launch (start us, length us, event | category | flops | bytes accessed | tf_op | source)
XLA Modules:
  0.0 176.9 jit_solution(17045224739113966874)
XLA Ops:
  6.6 0.7 all-gather.3.cloned.1.call-update
  7.3 0.7 all-gather.5.cloned.1.call-update
  8.0 1.1 convert_reduce_fusion
  9.2 1.2 fusion.15
  10.4 1.3 fusion.17
  11.7 4.3 %collective-permute-start = (bf16[15,1536]{1,0:T(8,128)(2,1)S(1)}, bf16[15,1536]{1,0:T(8,128)(2,1)S(1)}, u32[]{:S(2)}, u32[]{:S(2)}) collective-permute-start(bf16[15,1536]{1,0:T(8,128)(2,1)S(1)} %get-tuple-element.38), channel_id=1, source_target_pairs={{0,1},{1,2},{2,3},{3,4},{4,5},{5,6},{6,7},{7,8},{8,9},{9,10},{10,1... | collective-permute-start | bytes 138248 | tf_op jit(solution)/shard_map/ppermute | solution.py:14
  16.0 1.3 collective-permute-start.1
  17.3 0.8 copy.26
  18.4 0.6 reduce-window.6
  19.0 0.2 slice_reduce_fusion
  19.5 1.4 slice_reduce_fusion.30
  21.0 1.9 %slice_reduce_fusion.31 = (f32[1536]{0:T(1024)S(1)}, f32[1536]{0:T(1024)S(1)}, f32[1536]{0:T(1024)S(1)}, f32[1536]{0:T(1024)S(1)}, f32[1536]{0:T(1024)S(1)}, /*i...) fusion(f32[31,1536]{1,0:T(8,128)} %param.12), kind=kLoop, calls=%fused_computation.145 | loop fusion | bytes 233472 | tf_op jit(solution)/shard_map/slice | solution.py:43
  23.0 4.3 %fusion.56 = (f32[128]{0:T(128)S(1)}, f32[128,1536]{1,0:T(8,128)S(1)}) fusion(f32[1536]{0:T(1024)S(1)} %copy-done.2, bf16[15,1536]{1,0:T(8,128)(2,1)S(1)} %collective-permute-done.1, bf16[128,1536]{1,0:T(8,128)(2,1)S(1)} %fusion.17, f32[1536]{0:T(1024)S(1)} %get-tuple-element.34, f32[1536]{0:T(1024)S(1)} %get-tuple-element.35, ...), kind=kLoop, calls=%fused_computation.158 | loop fusion | flops 37552000 | bytes 1868288 | tf_op jit(solution)/shard_map/reduce_sum | solution.py:23
  27.4 0.2 multiply_reduce_fusion.1
  27.6 0.7 convolution_convert_fusion
  28.3 54.0 %all_to_all.10 = bf16[32,16,1536]{2,1,0:T(8,128)(2,1)S(1)} all-to-all(bf16[32,16,1536]{2,1,0:T(8,128)(2,1)S(1)} %bitcast.66), channel_id=1, replica_groups=mesh['fsdp'=16,'expert'=32] {'expert'}, dimensions={0} | all-to-all | bytes 3145728 | tf_op jit(solution)/shard_map/all_to_all | solution.py:62
  82.2 21.9 %all-gather.5.cloned.1.call-done = bf16[1,1536,1536]{2,1,0:T(8,128)(2,1)} async-done(((bf16[1,96,1536]{2,1,0:T(8,128)(2,1)}), bf16[1,1536,1536]{2,1,0:T(8,128)(2,1)}) %all-gather.5.cloned.1.call-update) | async-done | bytes 4718608 | tf_op jit(solution)/shard_map/all_gather | solution.py:60
  104.1 10.3 %fusion.4 = bf16[512,1536]{1,0:T(8,128)(2,1)} fusion(bf16[1,1536,1536]{2,1,0:T(8,128)(2,1)} %all-gather.5.cloned.1.call-done, bf16[512,1536]{1,0:T(8,128)(2,1)S(1)} %bitcast.68, bf16[1,1536,1536]{2,1,0:T(8,128)(2,1)} %all-gather.3.cloned.1.call-done), kind=kOutput, calls=%fused_computation.6 | convolution fusion | flops 4836556800 | bytes 12582912 | tf_op jit(solution)/shard_map/dot_general | solution.py:67
  114.4 10.5 %all-to-all-start.1 = ((bf16[32,16,1536]{2,1,0:T(8,128)(2,1)}), bf16[32,16,1536]{2,1,0:T(8,128)(2,1)S(1)}, u32[]{:S(2)}, u32[]{:S(2)}) async-start(bf16[32,16,1536]{2,1,0:T(8,128)(2,1)} %bitcast.67), calls=%async_computation.1 | async-start | bytes 3145728 | tf_op jit(solution)/shard_map/all_to_all | solution.py:68
  125.7 38.9 %all-to-all-done.1 = bf16[32,16,1536]{2,1,0:T(8,128)(2,1)S(1)} async-done(((bf16[32,16,1536]{2,1,0:T(8,128)(2,1)}), bf16[32,16,1536]{2,1,0:T(8,128)(2,1)S(1)}, u32[]{:S(2)}, u32[]{:S(2)}) %all-to-all-start.1) | async-done | bytes 1572896 | tf_op jit(solution)/shard_map/all_to_all | solution.py:68
  164.5 1.3 gather_fusion
  165.8 0.3 gather.7
  166.1 3.1 %multiply_reduce_fusion = f32[128,1536]{1,0:T(8,128)S(1)} fusion(bf16[128,2,1536]{2,1,0:T(2,128)(2,1)S(1)} %gather.7, pred[128,2]{1,0:T(8,128)(4,1)S(1)} %copy.30, f32[128,2]{1,0:T(8,128)S(1)} %copy.25), kind=kLoop, calls=%fused_computation.36 | loop fusion | flops 1376256 | bytes 1574144 | tf_op jit(solution)/shard_map/reduce_sum | solution.py:77
  169.2 0.8 fusion.19
  (41 shorter events, 1.6 us)
Async XLA Ops:
  6.5 16.4 %copy-start = (bf16[1,128,1536]{2,1,0:T(8,128)(2,1)S(1)}, bf16[1,128,1536]{2,1,0:T(8,128)(2,1)}, u32[]{:S(2)}) copy-start(bf16[1,128,1536]{2,1,0:T(8,128)(2,1)} %param.10) | copy-start | bytes 1179652
  6.5 16.3 %copy-start.1 = (s32[1,128,2]{1,2,0:T(2,128)S(1)}, s32[1,128,2]{1,2,0:T(2,128)}, u32[]{:S(2)}) copy-start(s32[1,128,2]{1,2,0:T(2,128)} %param.16) | copy-start | bytes 3076
  6.5 16.4 %copy-start.3 = (f32[1536]{0:T(1024)S(1)}, f32[1536]{0:T(1024)}, u32[]{:S(2)}) copy-start(f32[1536]{0:T(1024)} %param.13) | copy-start | bytes 18436
  6.5 16.4 %copy-start.2 = (f32[1536]{0:T(1024)S(1)}, f32[1536]{0:T(1024)}, u32[]{:S(2)}) copy-start(f32[1536]{0:T(1024)} %param.14) | copy-start | bytes 18436
  6.5 21.0 %copy-start.4 = (f32[1536]{0:T(1024)S(1)}, f32[1536]{0:T(1024)}, u32[]{:S(2)}) copy-start(f32[1536]{0:T(1024)} %param.15) | copy-start | bytes 18436
  6.5 75.7 %all-gather.3.cloned.1.call-start = ((), (), s32[]{:S(2)}) async-start(), calls=%async_computation.2 | async-start | bytes 5013504 | tf_op jit(solution)/shard_map/all_gather | solution.py:59
  7.3 96.8 %all-gather.5.cloned.1.call-start = ((), (), s32[]{:S(2)}) async-start(), calls=%async_computation.3 | async-start | bytes 5013504 | tf_op jit(solution)/shard_map/all_gather | solution.py:60
  11.7 11.2 %collective-permute-start = (bf16[15,1536]{1,0:T(8,128)(2,1)S(1)}, bf16[15,1536]{1,0:T(8,128)(2,1)S(1)}, u32[]{:S(2)}, u32[]{:S(2)}) collective-permute-start(bf16[15,1536]{1,0:T(8,128)(2,1)S(1)} %get-tuple-element.38), channel_id=1, source_target_pairs={{0,1},{1,2},{2,3},{3,4},{4,5},{5,6},{6,7},{7,8},{8,9},{9,10},{10,1... | collective-permute-start | bytes 138248 | tf_op jit(solution)/shard_map/ppermute | solution.py:14
  16.0 6.9 %collective-permute-start.1 = (bf16[15,1536]{1,0:T(8,128)(2,1)S(1)}, bf16[15,1536]{1,0:T(8,128)(2,1)S(1)}, u32[]{:S(2)}, u32[]{:S(2)}) collective-permute-start(bf16[15,1536]{1,0:T(8,128)(2,1)S(1)} %get-tuple-element.39), channel_id=1, source_target_pairs={{1,0},{2,1},{3,2},{4,3},{5,4},{6,5},{7,6},{8,7},{9,8},{10,9},{11,1... | collective-permute-start | bytes 138248 | tf_op jit(solution)/shard_map/ppermute | solution.py:17
  114.4 11.1 %copy-start.5 = (f32[1,128,2]{1,2,0:T(2,128)S(1)}, f32[1,128,2]{1,2,0:T(2,128)}, u32[]{:S(2)}) copy-start(f32[1,128,2]{1,2,0:T(2,128)} %param.17) | copy-start | bytes 3076
  114.4 50.1 %all-to-all-start.1 = ((bf16[32,16,1536]{2,1,0:T(8,128)(2,1)}), bf16[32,16,1536]{2,1,0:T(8,128)(2,1)S(1)}, u32[]{:S(2)}, u32[]{:S(2)}) async-start(bf16[32,16,1536]{2,1,0:T(8,128)(2,1)} %bitcast.67), calls=%async_computation.1 | async-start | bytes 3145728 | tf_op jit(solution)/shard_map/all_to_all | solution.py:68
Sparse Core Ops, SparseCore 0:
  9.5 48.9 all-gather.2
  60.5 43.5 all-gather.4
where the time goes:
time: 177 us
  waiting for transfers between devices  62.1 us (35%)
  blocking collectives  54 us (31%)
  starting transfers between devices  16.1 us (9%)
  between operations  13.6 us (8%)
  other arithmetic  13 us (7%)
  matrix products  10.9 us (6%)
  local copies, waits for them, and re-layouts  7.04 us (4%)
    all_to_all x1, blocking collectives, shards(): lax.all_to_all(outgoing, 'expert', split_axis=0, concat_axis=0, tiled=True)  54 us
    all_to_all x1, waiting for transfers between devices, shards(): lax.all_to_all(result.reshape(block.shape), 'expert', split_axis=0, conca...  38.9 us
    all_gather x1, waiting for transfers between devices, shards(): lax.all_gather(w_out, 'fsdp', axis=1, tiled=True)  21.9 us
    all_to_all x1, starting transfers between devices, shards(): lax.all_to_all(result.reshape(block.shape), 'expert', split_axis=0, conca...  10.5 us
    dot_general x1, matrix products, shards(): jnp.dot(hidden, full_out[0], preferred_element_type=jnp.float32)  10.3 us
    reduce_sum x2, other arithmetic, layer_norm(): centre = jnp.mean(values, axis=-1, keepdims=True)  5.48 us
    ppermute x1, starting transfers between devices, padded_2(): lax.ppermute(lax.slice_in_dim(block, block.shape[dim] - width, None, axis...  4.28 us
  transfers between devices with their start and end apart: 5, of which 2 were waited for; matrix products, arithmetic and copies ran while one was open for 9% of the time, Pallas kernels for 0%

commit v1 on v0

--- a/solution.py
+++ b/solution.py
@@ -4,6 +4,15 @@
 from jax.sharding import PartitionSpec as P
 
 eps_norm = 1e-05
+pair_pieces_all = lambda axis_id, local_block: jnp.concatenate(
+    lax.all_to_all(
+        jnp.stack([local_block for _ in range(lax.axis_size(axis_id))], axis=0),
+        axis_name=axis_id,
+        split_axis=0,
+        concat_axis=0,
+    ),
+    axis=1,
+)
 
 
 def padded_2(block, sides, width):
@@ -57,7 +66,7 @@
     outgoing = outgoing.astype(jnp.bfloat16).reshape(experts_all, capacity, width)
     full_in, full_out = (
         lax.all_gather(w_in, "fsdp", axis=1, tiled=True),
-        lax.all_gather(w_out, "fsdp", axis=1, tiled=True),
+        pair_pieces_all("fsdp", w_out),
     )
     block = lax.all_to_all(outgoing, "expert", split_axis=0, concat_axis=0, tiled=True)
     rows_in = block.reshape(-1, width)

time: 177 us -> 287 us (1.62)
  the two profiles are of different devices: /device:TPU:8 before, /device:TPU:24 now
where the time goes in v1:
time: 287 us
  waiting for transfers between devices  166 us (58%)
  blocking collectives  54 us (19%)
  starting transfers between devices  17.9 us (6%)
  other arithmetic  14.6 us (5%)
  between operations  13.6 us (5%)
  matrix products  10.9 us (4%)
  local copies, waits for them, and re-layouts  9.89 us (3%)
    all_to_all x1, waiting for transfers between devices, lax.all_to_all(jnp.stack([local_block for _ in range(lax.axis_size(axis_i...  126 us
    all_to_all x1, blocking collectives, shards(): lax.all_to_all(outgoing, 'expert', split_axis=0, concat_axis=0, tiled=True)  54 us
    all_to_all x1, waiting for transfers between devices, shards(): lax.all_to_all(result.reshape(block.shape), 'expert', split_axis=0, conca...  38.8 us
    dot_general x1, matrix products, shards(): jnp.dot(hidden, full_out[0], preferred_element_type=jnp.float32)  10.3 us
    all_to_all x1, starting transfers between devices, lax.all_to_all(jnp.stack([local_block for _ in range(lax.axis_size(axis_i...  7.35 us
    reduce_sum x2, other arithmetic, layer_norm(): centre = jnp.mean(values, axis=-1, keepdims=True)  6.34 us
  transfers between devices with their start and end apart: 5, of which 2 were waited for; matrix products, arithmetic and copies ran while one was open for 2% of the time, Pallas kernels for 0%

profile of v1, /device:TPU:24, one launch (start us, length us, event | category | flops | bytes accessed | tf_op | source)
XLA Modules:
  0.0 286.8 jit_solution(11505619480484774241)
XLA Ops:
  6.5 1.2 convert_reduce_fusion
  7.7 1.2 fusion.10
  9.0 1.3 fusion.12
  10.3 4.3 %collective-permute-start = (bf16[15,1536]{1,0:T(8,128)(2,1)S(1)}, bf16[15,1536]{1,0:T(8,128)(2,1)S(1)}, u32[]{:S(2)}, u32[]{:S(2)}) collective-permute-start(bf16[15,1536]{1,0:T(8,128)(2,1)S(1)} %get-tuple-element.38), channel_id=1, source_target_pairs={{0,1},{1,2},{2,3},{3,4},{4,5},{5,6},{6,7},{7,8},{8,9},{9,10},{10,1... | collective-permute-start | bytes 138248 | tf_op jit(solution)/shard_map/ppermute | solution.py:23
  14.6 1.3 collective-permute-start.1
  15.9 1.9 slice_reduce_fusion.31
  17.8 1.5 slice_reduce_fusion.30
  19.4 0.8 copy.26
  20.4 0.6 reduce-window.6
  21.6 0.7 broadcast_multiply_fusion
  22.4 5.1 %fusion.51 = (f32[128]{0:T(128)S(1)}, f32[128,1536]{1,0:T(8,128)S(1)}) fusion(f32[1536]{0:T(1024)} %param.14, bf16[15,1536]{1,0:T(8,128)(2,1)S(1)} %collective-permute-done.1, bf16[128,1536]{1,0:T(8,128)(2,1)S(1)} %fusion.12, f32[1536]{0:T(1024)S(1)} %get-tuple-element.34, f32[1536]{0:T(1024)S(1)} %get-tuple-element.35, f32[1536]{0:T(1024)S(1)} %get-tuple-element.6, ...), kind=kLoop, calls=%fused_computation.156 | loop fusion | flops 37552000 | bytes 1868288 | tf_op jit(solution)/shard_map/reduce_sum | solution.py:32
  27.8 0.7 convolution_convert_fusion.1
  28.5 54.0 %all_to_all.15 = bf16[32,16,1536]{2,1,0:T(8,128)(2,1)S(1)} all-to-all(bf16[32,16,1536]{2,1,0:T(8,128)(2,1)S(1)} %bitcast.64), channel_id=1, replica_groups=mesh['fsdp'=16,'expert'=32] {'expert'}, dimensions={0} | all-to-all | bytes 3145728 | tf_op jit(solution)/shard_map/all_to_all | solution.py:71
  82.4 2.7 stack.2
  85.1 7.4 %all-to-all-start.1 = ((bf16[16,1,96,1536]{3,2,1,0:T(8,128)(2,1)}), bf16[16,1,96,1536]{3,2,1,0:T(8,128)(2,1)}, u32[]{:S(2)}, u32[]{:S(2)}) async-start(bf16[16,1,96,1536]{3,2,1,0:T(8,128)(2,1)} %stack.2), calls=%async_computation.1 | async-start | bytes 9437184 | tf_op jit(solution)/shard_map/all_to_all | solution.py:8
  92.5 0.7 all-gather.2.cloned.1.call-update
  93.2 126.3 %all-to-all-done.1 = bf16[16,1,96,1536]{3,2,1,0:T(8,128)(2,1)} async-done(((bf16[16,1,96,1536]{3,2,1,0:T(8,128)(2,1)}), bf16[16,1,96,1536]{3,2,1,0:T(8,128)(2,1)}, u32[]{:S(2)}, u32[]{:S(2)}) %all-to-all-start.1) | async-done | bytes 4718624 | tf_op jit(solution)/shard_map/all_to_all | solution.py:8
  219.6 10.3 %convolution_convert_fusion = bf16[512,1536]{1,0:T(8,128)(2,1)} fusion(bf16[1536,1536]{1,0:T(8,128)(2,1)} %bitcast.9, bf16[512,1536]{1,0:T(8,128)(2,1)S(1)} %bitcast.66, bf16[1,1536,1536]{2,1,0:T(8,128)(2,1)} %all-gather.2.cloned.1.call-done), kind=kOutput, calls=%fused_computation.4 | convolution fusion | flops 4836556800 | bytes 12582912 | tf_op jit(solution)/shard_map/dot_general | solution.py:76
  229.8 5.0 %all-to-all-start.2 = ((bf16[32,16,1536]{2,1,0:T(8,128)(2,1)}), bf16[32,16,1536]{2,1,0:T(8,128)(2,1)S(1)}, u32[]{:S(2)}, u32[]{:S(2)}) async-start(bf16[32,16,1536]{2,1,0:T(8,128)(2,1)} %bitcast.65), calls=%async_computation.2 | async-start | bytes 3145728 | tf_op jit(solution)/shard_map/all_to_all | solution.py:77
  235.6 38.8 %all-to-all-done.2 = bf16[32,16,1536]{2,1,0:T(8,128)(2,1)S(1)} async-done(((bf16[32,16,1536]{2,1,0:T(8,128)(2,1)}), bf16[32,16,1536]{2,1,0:T(8,128)(2,1)S(1)}, u32[]{:S(2)}, u32[]{:S(2)}) %all-to-all-start.2) | async-done | bytes 1572896 | tf_op jit(solution)/shard_map/all_to_all | solution.py:77
  274.4 1.3 gather_fusion
  275.7 0.3 gather.7
  276.0 3.1 %multiply_reduce_fusion = f32[128,1536]{1,0:T(8,128)S(1)} fusion(bf16[128,2,1536]{2,1,0:T(2,128)(2,1)S(1)} %gather.7, pred[128,2]{1,0:T(8,128)(4,1)S(1)} %copy.30, f32[128,2]{1,0:T(8,128)S(1)} %copy.25), kind=kLoop, calls=%fused_computation.34 | loop fusion | flops 1376256 | bytes 1574144 | tf_op jit(solution)/shard_map/reduce_sum | solution.py:86
  279.1 0.8 fusion.14
  (39 shorter events, 1.9 us)
Async XLA Ops:
  6.5 15.8 %copy-start = (bf16[1,128,1536]{2,1,0:T(8,128)(2,1)S(1)}, bf16[1,128,1536]{2,1,0:T(8,128)(2,1)}, u32[]{:S(2)}) copy-start(bf16[1,128,1536]{2,1,0:T(8,128)(2,1)} %param.10) | copy-start | bytes 1179652
  6.5 21.3 %copy-start.3 = (f32[1536]{0:T(1024)S(1)}, f32[1536]{0:T(1024)}, u32[]{:S(2)}) copy-start(f32[1536]{0:T(1024)} %param.15) | copy-start | bytes 18436
  10.3 12.0 %collective-permute-start = (bf16[15,1536]{1,0:T(8,128)(2,1)S(1)}, bf16[15,1536]{1,0:T(8,128)(2,1)S(1)}, u32[]{:S(2)}, u32[]{:S(2)}) collective-permute-start(bf16[15,1536]{1,0:T(8,128)(2,1)S(1)} %get-tuple-element.38), channel_id=1, source_target_pairs={{0,1},{1,2},{2,3},{3,4},{4,5},{5,6},{6,7},{7,8},{8,9},{9,10},{10,1... | collective-permute-start | bytes 138248 | tf_op jit(solution)/shard_map/ppermute | solution.py:23
  14.6 7.8 %collective-permute-start.1 = (bf16[15,1536]{1,0:T(8,128)(2,1)S(1)}, bf16[15,1536]{1,0:T(8,128)(2,1)S(1)}, u32[]{:S(2)}, u32[]{:S(2)}) collective-permute-start(bf16[15,1536]{1,0:T(8,128)(2,1)S(1)} %get-tuple-element.39), channel_id=1, source_target_pairs={{1,0},{2,1},{3,2},{4,3},{5,4},{6,5},{7,6},{8,7},{9,8},{10,9},{11,1... | collective-permute-start | bytes 138248 | tf_op jit(solution)/shard_map/ppermute | solution.py:26
  27.5 54.9 %copy-start.1 = (bf16[1,96,1536]{2,1,0:T(8,128)(2,1)S(1)}, bf16[1,96,1536]{2,1,0:T(8,128)(2,1)}, u32[]{:S(2)}) copy-start(bf16[1,96,1536]{2,1,0:T(8,128)(2,1)} %param.19) | copy-start | bytes 884740
  85.1 134.4 %all-to-all-start.1 = ((bf16[16,1,96,1536]{3,2,1,0:T(8,128)(2,1)}), bf16[16,1,96,1536]{3,2,1,0:T(8,128)(2,1)}, u32[]{:S(2)}, u32[]{:S(2)}) async-start(bf16[16,1,96,1536]{3,2,1,0:T(8,128)(2,1)} %stack.2), calls=%async_computation.1 | async-start | bytes 9437184 | tf_op jit(solution)/shard_map/all_to_all | solution.py:8
  92.5 127.1 %all-gather.2.cloned.1.call-start = ((), (), s32[]{:S(2)}) async-start(), calls=%async_computation.3 | async-start | bytes 5013504 | tf_op jit(solution)/shard_map/all_gather | solution.py:68
  229.8 5.4 %copy-start.2 = (s32[1,128,2]{1,2,0:T(2,128)S(1)}, s32[1,128,2]{1,2,0:T(2,128)}, u32[]{:S(2)}) copy-start(s32[1,128,2]{1,2,0:T(2,128)} %param.16) | copy-start | bytes 3076
  229.8 5.6 %copy-start.4 = (f32[1,128,2]{1,2,0:T(2,128)S(1)}, f32[1,128,2]{1,2,0:T(2,128)}, u32[]{:S(2)}) copy-start(f32[1,128,2]{1,2,0:T(2,128)} %param.17) | copy-start | bytes 3076
  229.8 44.6 %all-to-all-start.2 = ((bf16[32,16,1536]{2,1,0:T(8,128)(2,1)}), bf16[32,16,1536]{2,1,0:T(8,128)(2,1)S(1)}, u32[]{:S(2)}, u32[]{:S(2)}) async-start(bf16[32,16,1536]{2,1,0:T(8,128)(2,1)} %bitcast.65), calls=%async_computation.2 | async-start | bytes 3145728 | tf_op jit(solution)/shard_map/all_to_all | solution.py:77
Sparse Core Ops, SparseCore 0:
  95.4 106.4 all-gather.1
